TPU v7x, 32 devices: a whole 2x2x4 slice. The times are simulated.
32 devices in a mesh: tile: 2 (over y), dom: 4 (over x, core), view: 4 (over z).
Axes of the slice: x: 2, y: 2, z: 4, core: 2. Of those that a mesh axis runs over, the one named last changes fastest.
Arguments:
- estimate: float32 [128, 32, 256], P(('tile', 'dom')), parts along dimension 0, may hold values from 0.25 to 4
- observed: float32 [4, 128, 32, 256], P('view', ('tile', 'dom')), parts along dimension 1, may hold values from 0.5 to 8
- psf: float32 [4, 4, 3, 9], P('view'), may hold values from 0.02 to 1
- src_map: int32 [4, 16], replicated, may hold values from 0 to 15, as said below
- depth_band: int32 [4, 64], P('view'), may hold values from 0 to 3, as said below
Outputs:
- new_estimate: float32 [128, 32, 256], P(('tile', 'dom')), parts along dimension 0
There are 2 independent parts, one for each index of `tile`. A program takes and returns all parts, laid end to end along the dimension named above; an argument that names none is the same for every part. Nothing has to cross between parts.
Inputs may be any that keep to these rules, and one draw needn't show every extreme that they name: For each view src_map is a permutation of the 16 joined blocks, and the 4 camera blocks f * 4 to f * 4 + 3 show blocks of 4 different depth slabs, one of each. For each view depth_band never falls along depth; it is 0 at the first plane and 3 at the last.
All inputs are finite; a program needn't handle non-finite values.
Results may differ from a plain program's by a relative error of at most 0.0001.
Values sent between devices are 32-bit elements; how exact they have to be, the bound alone decides.
No kernel may reach another device: no remote copies, remote signals or barrier semaphores. Data moves between devices by JAX's collectives and lax.ppermute only.
A program may use at most 64 MiB of HBM per device.

v0:
```python
import jax
import jax.numpy as jnp
from jax import lax
from jax.sharding import PartitionSpec as P

RADIUS = 4
precise = lax.Precision.HIGHEST


def extended_2(shard, sides, width):
    for axis, dim in sides:
        size, length = (lax.axis_size(axis), shard.shape[dim])
        up = [(i, (i + 1) % size) for i in range(size - 1)]
        down = [(j, i) for i, j in up]
        last = lax.slice_in_dim(shard, length - width, length, axis=dim)
        initial = lax.slice_in_dim(shard, 0, width, axis=dim)
        before = lax.ppermute(last, axis, up)
        after = lax.ppermute(initial, axis, down)
        shard = jnp.concatenate([before, shard, after], axis=dim)
    return shard


def taps_along(field, taps, axis, flipped):
    tap_count = taps.shape[1]
    reach = (tap_count - 1) // 2
    length = field.shape[axis]
    widths = [(0, 0), (0, 0), (0, 0)]
    widths[axis] = (reach, reach)
    padded = jnp.pad(field, widths)
    total = jnp.zeros(field.shape, jnp.float32)
    for offset in range(tap_count):
        start = 2 * reach - offset if flipped else offset
        piece = lax.slice_in_dim(padded, start, start + length, axis=axis)
        total = total + taps[:, offset][:, None, None] * piece
    return total


def lateral_fwd(field, x_taps, y_taps):
    inner = taps_along(field, x_taps, 2, False)
    return taps_along(inner, y_taps, 1, False)


def lateral_back(field, x_taps, y_taps):
    inner = taps_along(field, y_taps, 1, True)
    return taps_along(inner, x_taps, 2, True)


def body(estimate, observed, psf, src_map, depth_band):
    plane_count, row_count, lane_count = estimate.shape
    block_count = lax.axis_size("dom")
    block_rows = row_count // block_count
    dom_index = lax.axis_index("dom")
    view_index = lax.axis_index("view")
    view_count = lax.axis_size("view")
    plane_start = dom_index * plane_count
    slot_ids = jnp.arange(block_count, dtype=jnp.int32)
    my_map = lax.dynamic_index_in_dim(src_map, view_index, 0, keepdims=False)
    grid_map = my_map.reshape(block_count, block_count)
    source_dev = grid_map // block_count
    source_slot = grid_map % block_count
    send_slot = jnp.sum(jnp.where(source_dev == dom_index, source_slot, 0), axis=1)
    blocks = estimate.reshape(plane_count, block_count, block_rows, lane_count)
    outgoing = jnp.take(blocks, send_slot, axis=1)
    arrived = lax.all_to_all(outgoing, "dom", split_axis=1, concat_axis=1, tiled=True)
    my_sources = lax.dynamic_index_in_dim(source_dev, dom_index, 0, keepdims=False)
    camera = jnp.take(arrived, my_sources, axis=1).reshape(plane_count, row_count, lane_count)
    kernels = psf[0]
    band_all = depth_band[0]
    total_planes = band_all.shape[0]
    reach = (kernels.shape[2] - 1) // 2
    ext_count = plane_count + 2 * reach
    ext_index = jnp.clip(
        plane_start - reach + jnp.arange(ext_count, dtype=jnp.int32), 0, total_planes - 1
    )
    band_ext = jnp.take(band_all, ext_index)
    band_own = lax.dynamic_slice_in_dim(band_all, plane_start, plane_count)
    x_own = jnp.take(kernels[:, 2], band_own, axis=0)
    y_own = jnp.take(kernels[:, 1], band_own, axis=0)
    lateral = lateral_fwd(camera, x_own, y_own)
    extended = extended_2(lateral, (("dom", 0),), RADIUS)
    z_pos = jnp.arange(plane_count, dtype=jnp.int32)[:, None]
    s_pos = jnp.arange(ext_count, dtype=jnp.int32)[None, :]
    fwd_tap = s_pos - z_pos
    fwd_valid = (fwd_tap >= 0) & (fwd_tap <= 2 * reach)
    taps_own = jnp.take(kernels[:, 0], band_own, axis=0)
    row_sel = jnp.broadcast_to(z_pos, (plane_count, ext_count))
    depth_fwd = jnp.where(fwd_valid, taps_own[row_sel, jnp.clip(fwd_tap, 0, 2 * reach)], 0.0)
    blurred = jnp.einsum("zs,syx->zyx", depth_fwd, extended, precision=precise)
    ratio_field = observed[0] / blurred
    ratio_ext = extended_2(ratio_field, (("dom", 0),), RADIUS)
    back_tap = z_pos - s_pos + 2 * reach
    back_valid = (back_tap >= 0) & (back_tap <= 2 * reach)
    taps_ext = jnp.take(kernels[:, 0], band_ext, axis=0)
    col_sel = jnp.broadcast_to(s_pos, (plane_count, ext_count))
    depth_back = jnp.where(back_valid, taps_ext[col_sel, jnp.clip(back_tap, 0, 2 * reach)], 0.0)
    zback = jnp.einsum("zs,syx->zyx", depth_back, ratio_ext, precision=precise)
    back = lateral_back(zback, x_own, y_own)
    dest_slot = jnp.sum(
        jnp.where(my_sources[None, :] == slot_ids[:, None], slot_ids[None, :], 0), axis=1
    )
    inverse_slot = jnp.sum(
        jnp.where(send_slot[None, :] == slot_ids[:, None], slot_ids[None, :], 0), axis=1
    )
    back_blocks = back.reshape(plane_count, block_count, block_rows, lane_count)
    returning = jnp.take(back_blocks, dest_slot, axis=1)
    returned = lax.all_to_all(returning, "dom", split_axis=1, concat_axis=1, tiled=True)
    log_corr = jnp.log(jnp.take(returned, inverse_slot, axis=1))
    log_total = lax.psum(log_corr, "view")
    updated = blocks * jnp.exp(log_total / view_count)
    return updated.reshape(plane_count, row_count, lane_count)


def solution(mesh):
    in_specs = (
        P(("tile", "dom"), None, None),
        P("view", ("tile", "dom"), None, None),
        P("view", None, None, None),
        P(),
        P("view", None),
    )
    out_specs = P(("tile", "dom"), None, None)
    return jax.shard_map(body, mesh=mesh, in_specs=in_specs, out_specs=out_specs, check_vma=False)
```

profile of v0, /device:TPU:0, one launch (start us, length us, event | category | flops | bytes accessed | tf_op | source)
XLA Modules:
  0.0 108.7 jit_solution(233660518752022189)
XLA Ops:
  6.5 0.7 copy-done
  7.6 1.6 %gather_fusion.7 = f32[4,16,8,256]{3,2,1,0:T(8,128)S(1)} fusion(f32[16,4,8,256]{3,2,1,0:T(8,128)} %bitcast.51, s32[1024]{0:T(1024)S(1)} %pad_clamp_fusion.3), kind=kCustom, calls=%fused_computation.1.clone | custom fusion | bytes 1048592 | tf_op jit(solution)/shard_map/jit(_take)/gather | solution.py:63
  9.2 0.9 select_bitcast_fusion.2
  10.2 4.2 %all-to-all-start = ((f32[16,4,8,256]{3,2,0,1:T(8,128)}), f32[16,4,8,256]{3,2,0,1:T(8,128)S(1)}, u32[]{:S(2)}, u32[]{:S(2)}) async-start(f32[16,4,8,256]{3,2,0,1:T(8,128)} %select_bitcast_fusion.2), calls=%async_computation | async-start | bytes 1048576 | tf_op jit(solution)/shard_map/all_to_all | solution.py:64
  14.4 0.6 copy-done.1
  15.1 0.7 gather_fusion
  15.9 0.6 copy-done.3
  16.5 0.6 gather_fusion.6
  17.1 0.6 gather_fusion.4
  17.7 0.6 gather_fusion.5
  18.3 0.6 gather_fusion.1
  18.9 0.5 slice_reduce_fusion.16
  19.4 3.8 %all-to-all-done = f32[16,4,8,256]{3,2,0,1:T(8,128)S(1)} async-done(((f32[16,4,8,256]{3,2,0,1:T(8,128)}), f32[16,4,8,256]{3,2,0,1:T(8,128)S(1)}, u32[]{:S(2)}, u32[]{:S(2)}) %all-to-all-start) | async-done | bytes 524320 | tf_op jit(solution)/shard_map/all_to_all | solution.py:64
  23.3 0.6 gather_fusion.8
  24.1 1.2 %fusion.51 = f32[16,32,256]{2,0,1:T(8,128)S(1)} fusion(f32[16,32,256]{2,0,1:T(8,128)S(1)} %bitcast.53, f32[16]{0:T(128)S(1)} %get-tuple-element.52, f32[16]{0:T(128)S(1)} %get-tuple-element.51, f32[16]{0:T(128)S(1)} %get-tuple-element.50, f32[16]{0:T(128)S(1)} %get-tuple-element.49, f32[16]{0:T(128)S(1)} %get-tuple-element.48, f32[16]{0:T(128)S(1)} %get-tuple-element.47, ...), kind=kLoop, calls=%fused_computation.95 | loop fusion | flops 2228224 | bytes 1049152 | tf_op jit(solution)/shard_map/add | solution.py:34
  25.7 1.3 %collective-permute-start = (f32[4,32,256]{2,0,1:T(4,128)S(1)}, f32[4,32,256]{2,0,1:T(4,128)S(1)}, u32[]{:S(2)}, u32[]{:S(2)}) collective-permute-start(f32[4,32,256]{2,0,1:T(4,128)S(1)} %get-tuple-element.33), channel_id=1, source_target_pairs={{0,4},{4,8},{8,12},{1,5},{5,9},{9,13},{2,6},{6,10},{10,14},{3,7},{... | collective-permute-start | bytes 393224 | tf_op jit(solution)/shard_map/ppermute | solution.py:17
  27.0 1.3 %collective-permute-start.1 = (f32[4,32,256]{2,0,1:T(4,128)S(1)}, f32[4,32,256]{2,0,1:T(4,128)S(1)}, u32[]{:S(2)}, u32[]{:S(2)}) collective-permute-start(f32[4,32,256]{2,0,1:T(4,128)S(1)} %get-tuple-element.34), channel_id=1, source_target_pairs={{4,0},{8,4},{12,8},{5,1},{9,5},{13,9},{6,2},{10,6},{14,10},{7,3},{... | collective-permute-start | bytes 393224 | tf_op jit(solution)/shard_map/ppermute | solution.py:18
  28.4 2.9 %gather_fusion.3 = f32[384]{0:T(512)S(1)} fusion(f32[16,9]{1,0:T(8,128)S(1)} %get-tuple-element.38, s32[384]{0:T(512)S(1)} %reshape.266), kind=kCustom, calls=%fused_computation.10 | custom fusion | bytes 6144 | tf_op jit(solution)/shard_map/gather | solution.py:87
  31.5 0.9 convolution_divide_fusion
  32.4 4.9 %collective-permute-start.2 = (f32[4,32,256]{2,0,1:T(4,128)S(1)}, f32[4,32,256]{2,0,1:T(4,128)S(1)}, u32[]{:S(2)}, u32[]{:S(2)}) collective-permute-start(f32[4,32,256]{2,0,1:T(4,128)S(1)} %get-tuple-element.31), channel_id=1, source_target_pairs={{0,4},{4,8},{8,12},{1,5},{5,9},{9,13},{2,6},{6,10},{10,14},{3,7},{... | collective-permute-start | bytes 393224 | tf_op jit(solution)/shard_map/ppermute | solution.py:17
  37.3 1.3 %collective-permute-start.3 = (f32[4,32,256]{2,0,1:T(4,128)S(1)}, f32[4,32,256]{2,0,1:T(4,128)S(1)}, u32[]{:S(2)}, u32[]{:S(2)}) collective-permute-start(f32[4,32,256]{2,0,1:T(4,128)S(1)} %get-tuple-element.32), channel_id=1, source_target_pairs={{4,0},{8,4},{12,8},{5,1},{9,5},{13,9},{6,2},{10,6},{14,10},{7,3},{... | collective-permute-start | bytes 393224 | tf_op jit(solution)/shard_map/ppermute | solution.py:18
  38.7 2.9 %gather_fusion.2 = f32[384]{0:T(512)S(1)} fusion(f32[24,9]{1,0:T(8,128)S(1)} %broadcast_select_fusion, s32[384]{0:T(512)S(1)} %reshape.260), kind=kCustom, calls=%fused_computation.9 | custom fusion | bytes 6144 | tf_op jit(solution)/shard_map/gather | solution.py:95
  41.8 0.7 fusion.5
  42.9 1.2 %fusion.67 = f32[16,32,256]{2,0,1:T(8,128)S(1)} fusion(f32[16,32,256]{2,0,1:T(8,128)S(1)} %fusion.35, f32[16]{0:T(128)S(1)} %get-tuple-element.52, f32[16]{0:T(128)S(1)} %get-tuple-element.51, f32[16]{0:T(128)S(1)} %get-tuple-element.50, f32[16]{0:T(128)S(1)} %get-tuple-element.49, f32[16]{0:T(128)S(1)} %get-tuple-element.48, f32[16]{0:T(128)S(1)} %get-tuple-element.47, ...), kind=kLoop, calls=%fused_computation.111 | loop fusion | flops 2228224 | bytes 1049152 | tf_op jit(solution)/shard_map/add | solution.py:34
  44.3 0.6 gather_fusion.9
  44.9 0.9 select_bitcast_fusion
  45.8 4.0 %all-to-all-start.1 = ((f32[16,4,8,256]{3,2,0,1:T(8,128)}), f32[16,4,8,256]{3,2,0,1:T(8,128)S(1)}, u32[]{:S(2)}, u32[]{:S(2)}) async-start(f32[16,4,8,256]{3,2,0,1:T(8,128)} %select_bitcast_fusion), calls=%async_computation.1 | async-start | bytes 1048576 | tf_op jit(solution)/shard_map/all_to_all | solution.py:106
  49.9 8.8 %all-to-all-done.1 = f32[16,4,8,256]{3,2,0,1:T(8,128)S(1)} async-done(((f32[16,4,8,256]{3,2,0,1:T(8,128)}), f32[16,4,8,256]{3,2,0,1:T(8,128)S(1)}, u32[]{:S(2)}, u32[]{:S(2)}) %all-to-all-start.1) | async-done | bytes 524320 | tf_op jit(solution)/shard_map/all_to_all | solution.py:106
  58.7 0.6 gather_fusion.10
  59.3 0.9 bitcast_log_fusion
  60.3 39.7 %all-reduce.6.cloned.1.call-done = f32[16,4,8,256]{3,2,1,0:T(8,128)} async-done(((f32[16,4,8,256]{3,2,1,0:T(8,128)}), f32[16,4,8,256]{3,2,1,0:T(8,128)}) %all-reduce.6.cloned.1.call-update) | async-done | bytes 524304 | tf_op jit(solution)/shard_map/psum | solution.py:108
  100.0 1.9 %multiply_bitcast_fusion = f32[16,32,256]{2,1,0:T(8,128)} fusion(f32[16,4,8,256]{3,2,1,0:T(8,128)} %all-reduce.6.cloned.1.call-done, f32[16,32,256]{2,1,0:T(8,128)S(1)} %copy-done.2), kind=kLoop, calls=%fused_computation.124 | loop fusion | flops 262144 | bytes 1572864 | tf_op jit(solution)/shard_map/reshape | solution.py:110
  (53 shorter events, 2.7 us)
Async XLA Ops:
  6.5 0.7 copy-start
  10.2 13.1 %all-to-all-start = ((f32[16,4,8,256]{3,2,0,1:T(8,128)}), f32[16,4,8,256]{3,2,0,1:T(8,128)S(1)}, u32[]{:S(2)}, u32[]{:S(2)}) async-start(f32[16,4,8,256]{3,2,0,1:T(8,128)} %select_bitcast_fusion.2), calls=%async_computation | async-start | bytes 1048576 | tf_op jit(solution)/shard_map/all_to_all | solution.py:64
  14.4 0.7 copy-start.1
  15.8 0.7 copy-start.3
  25.7 5.7 %collective-permute-start = (f32[4,32,256]{2,0,1:T(4,128)S(1)}, f32[4,32,256]{2,0,1:T(4,128)S(1)}, u32[]{:S(2)}, u32[]{:S(2)}) collective-permute-start(f32[4,32,256]{2,0,1:T(4,128)S(1)} %get-tuple-element.33), channel_id=1, source_target_pairs={{0,4},{4,8},{8,12},{1,5},{5,9},{9,13},{2,6},{6,10},{10,14},{3,7},{... | collective-permute-start | bytes 393224 | tf_op jit(solution)/shard_map/ppermute | solution.py:17
  27.0 4.4 %collective-permute-start.1 = (f32[4,32,256]{2,0,1:T(4,128)S(1)}, f32[4,32,256]{2,0,1:T(4,128)S(1)}, u32[]{:S(2)}, u32[]{:S(2)}) collective-permute-start(f32[4,32,256]{2,0,1:T(4,128)S(1)} %get-tuple-element.34), channel_id=1, source_target_pairs={{4,0},{8,4},{12,8},{5,1},{9,5},{13,9},{6,2},{10,6},{14,10},{7,3},{... | collective-permute-start | bytes 393224 | tf_op jit(solution)/shard_map/ppermute | solution.py:18
  28.4 3.0 %copy-start.4 = (f32[1,16,32,256]{3,2,1,0:T(8,128)S(1)}, f32[1,16,32,256]{3,2,1,0:T(8,128)}, u32[]{:S(2)}) copy-start(f32[1,16,32,256]{3,2,1,0:T(8,128)} %param.10) | copy-start | bytes 1572868
  32.4 9.4 %collective-permute-start.2 = (f32[4,32,256]{2,0,1:T(4,128)S(1)}, f32[4,32,256]{2,0,1:T(4,128)S(1)}, u32[]{:S(2)}, u32[]{:S(2)}) collective-permute-start(f32[4,32,256]{2,0,1:T(4,128)S(1)} %get-tuple-element.31), channel_id=1, source_target_pairs={{0,4},{4,8},{8,12},{1,5},{5,9},{9,13},{2,6},{6,10},{10,14},{3,7},{... | collective-permute-start | bytes 393224 | tf_op jit(solution)/shard_map/ppermute | solution.py:17
  37.3 4.5 %collective-permute-start.3 = (f32[4,32,256]{2,0,1:T(4,128)S(1)}, f32[4,32,256]{2,0,1:T(4,128)S(1)}, u32[]{:S(2)}, u32[]{:S(2)}) collective-permute-start(f32[4,32,256]{2,0,1:T(4,128)S(1)} %get-tuple-element.32), channel_id=1, source_target_pairs={{4,0},{8,4},{12,8},{5,1},{9,5},{13,9},{6,2},{10,6},{14,10},{7,3},{... | collective-permute-start | bytes 393224 | tf_op jit(solution)/shard_map/ppermute | solution.py:18
  45.8 12.8 %all-to-all-start.1 = ((f32[16,4,8,256]{3,2,0,1:T(8,128)}), f32[16,4,8,256]{3,2,0,1:T(8,128)S(1)}, u32[]{:S(2)}, u32[]{:S(2)}) async-start(f32[16,4,8,256]{3,2,0,1:T(8,128)} %select_bitcast_fusion), calls=%async_computation.1 | async-start | bytes 1048576 | tf_op jit(solution)/shard_map/all_to_all | solution.py:106
  49.9 50.1 %all-reduce.6.cloned.1.call-start = ((), (), s32[]{:S(2)}) async-start(), calls=%async_computation.2 | async-start | bytes 1048576 | tf_op jit(solution)/shard_map/psum | solution.py:108
  60.3 39.7 %copy-start.2 = (f32[16,32,256]{2,1,0:T(8,128)S(1)}, f32[16,32,256]{2,1,0:T(8,128)}, u32[]{:S(2)}) copy-start(f32[16,32,256]{2,1,0:T(8,128)} %param.9) | copy-start | bytes 1572868
Sparse Core Ops, SparseCore 0:
  60.4 39.5 all-reduce.5
where the time goes:
time: 109 us
  waiting for transfers between devices  52.3 us (48%)
  starting transfers between devices  17 us (16%)
  local copies, waits for them, and re-layouts  15.6 us (14%)
  between operations  13.7 us (13%)
  other arithmetic  8.56 us (8%)
  matrix products  1.56 us (1%)
    psum x1, waiting for transfers between devices, body(): log_total = lax.psum(log_corr, 'view')  39.7 us
    all_to_all x1, waiting for transfers between devices, body(): lax.all_to_all(returning, 'dom', split_axis=1, concat_axis=1, tiled=True)  8.78 us
    ppermute x2, starting transfers between devices, extended_2(): before = lax.ppermute(last, axis, up)  6.17 us
    all_to_all x1, starting transfers between devices, body(): lax.all_to_all(outgoing, 'dom', split_axis=1, concat_axis=1, tiled=True)  4.24 us
    all_to_all x1, starting transfers between devices, body(): lax.all_to_all(returning, 'dom', split_axis=1, concat_axis=1, tiled=True)  4.03 us
    all_to_all x1, waiting for transfers between devices, body(): lax.all_to_all(outgoing, 'dom', split_axis=1, concat_axis=1, tiled=True)  3.78 us
    add x4, other arithmetic, taps_along(): total = total + taps[:, offset][:, None, None] * piece  3.03 us
    gather x2, local copies, waits for them, and re-layouts, body(): taps_ext[col_sel, jnp.clip(back_tap, 0, 2 * reach)]  2.96 us
  transfers between devices with their start and end apart: 7, of which 3 were waited for; matrix products, arithmetic and copies ran while one was open for 9% of the time, Pallas kernels for 0%

commit v1 on v0

--- a/solution.py
+++ b/solution.py
@@ -105,7 +105,7 @@
     returning = jnp.take(back_blocks, dest_slot, axis=1)
     returned = lax.all_to_all(returning, "dom", split_axis=1, concat_axis=1, tiled=True)
     log_corr = jnp.log(jnp.take(returned, inverse_slot, axis=1))
-    log_total = lax.psum(log_corr, "view")
+    log_total = jnp.sum(lax.all_gather(log_corr, "view"), axis=0)
     updated = blocks * jnp.exp(log_total / view_count)
     return updated.reshape(plane_count, row_count, lane_count)
 

time: 109 us -> 117 us (1.073)
  waiting for transfers between devices: 52.3 us -> 60.6 us
  local copies, waits for them, and re-layouts: 15.6 us -> 14 us
  other arithmetic: 8.56 us -> 9.75 us
    all_gather x0 -> x1, waiting for transfers between devices: none -> 46.8 us  [body(): log_total = jnp.sum(lax.all_gather(log_corr, 'view'), axis=0)]
    psum x1 -> x0, waiting for transfers between devices: 39.7 us -> none  [body(): log_total = lax.psum(log_corr, 'view')]
    reshape x1 -> x0, other arithmetic: 1.93 us -> none  [body(): return updated.reshape(plane_count, row_count, lane_count)]
    reduce_sum x0 -> x1, other arithmetic: none -> 1.9 us  [body(): log_total = jnp.sum(lax.all_gather(log_corr, 'view'), axis=0)]
    unnamed x10, local copies, waits for them, and re-layouts: 1.94 us -> 0.69 us
    all_to_all x1, waiting for transfers between devices: 3.78 us -> 5.01 us  [body(): lax.all_to_all(outgoing, 'dom', split_axis=1, concat_axis=1, tiled=True)]
where the time goes in v1:
time: 117 us
  waiting for transfers between devices  60.6 us (52%)
  starting transfers between devices  17 us (15%)
  local copies, waits for them, and re-layouts  14 us (12%)
  between operations  13.8 us (12%)
  other arithmetic  9.75 us (8%)
  matrix products  1.53 us (1%)
    all_gather x1, waiting for transfers between devices, body(): log_total = jnp.sum(lax.all_gather(log_corr, 'view'), axis=0)  46.8 us
    all_to_all x1, waiting for transfers between devices, body(): lax.all_to_all(returning, 'dom', split_axis=1, concat_axis=1, tiled=True)  8.78 us
    ppermute x2, starting transfers between devices, extended_2(): before = lax.ppermute(last, axis, up)  6.17 us
    all_to_all x1, waiting for transfers between devices, body(): lax.all_to_all(outgoing, 'dom', split_axis=1, concat_axis=1, tiled=True)  5.01 us
    all_to_all x1, starting transfers between devices, body(): lax.all_to_all(outgoing, 'dom', split_axis=1, concat_axis=1, tiled=True)  4.24 us
    all_to_all x1, starting transfers between devices, body(): lax.all_to_all(returning, 'dom', split_axis=1, concat_axis=1, tiled=True)  4.03 us
    add x4, other arithmetic, taps_along(): total = total + taps[:, offset][:, None, None] * piece  3.03 us
    gather x2, local copies, waits for them, and re-layouts, body(): taps_own[row_sel, jnp.clip(fwd_tap, 0, 2 * reach)]  2.96 us
  transfers between devices with their start and end apart: 7, of which 3 were waited for; matrix products, arithmetic and copies ran while one was open for 9% of the time, Pallas kernels for 0%

profile of v1, /device:TPU:0, one launch (start us, length us, event | category | flops | bytes accessed | tf_op | source)
XLA Modules:
  0.0 116.7 jit_solution(12324306947393694395)
XLA Ops:
  6.5 0.7 copy-done
  7.6 1.6 %gather_fusion.7 = f32[4,16,8,256]{3,2,1,0:T(8,128)S(1)} fusion(f32[16,4,8,256]{3,2,1,0:T(8,128)} %bitcast.51, s32[1024]{0:T(1024)S(1)} %pad_clamp_fusion.3), kind=kCustom, calls=%fused_computation.1.clone | custom fusion | bytes 1048592 | tf_op jit(solution)/shard_map/jit(_take)/gather | solution.py:63
  9.2 0.9 select_bitcast_fusion.2
  10.2 4.2 %all-to-all-start = ((f32[16,4,8,256]{3,2,0,1:T(8,128)}), f32[16,4,8,256]{3,2,0,1:T(8,128)S(1)}, u32[]{:S(2)}, u32[]{:S(2)}) async-start(f32[16,4,8,256]{3,2,0,1:T(8,128)} %select_bitcast_fusion.2), calls=%async_computation | async-start | bytes 1048576 | tf_op jit(solution)/shard_map/all_to_all | solution.py:64
  14.4 0.7 gather_fusion
  15.3 0.6 gather_fusion.5
  15.9 0.6 gather_fusion.4
  16.4 0.6 gather_fusion.6
  17.1 0.6 gather_fusion.1
  17.6 0.5 slice_reduce_fusion.16
  18.2 5.0 %all-to-all-done = f32[16,4,8,256]{3,2,0,1:T(8,128)S(1)} async-done(((f32[16,4,8,256]{3,2,0,1:T(8,128)}), f32[16,4,8,256]{3,2,0,1:T(8,128)S(1)}, u32[]{:S(2)}, u32[]{:S(2)}) %all-to-all-start) | async-done | bytes 524320 | tf_op jit(solution)/shard_map/all_to_all | solution.py:64
  23.3 0.6 gather_fusion.8
  24.1 1.2 fusion.51
  25.3 0.4 fusion.19
  25.7 1.3 %collective-permute-start = (f32[4,32,256]{2,0,1:T(4,128)S(1)}, f32[4,32,256]{2,0,1:T(4,128)S(1)}, u32[]{:S(2)}, u32[]{:S(2)}) collective-permute-start(f32[4,32,256]{2,0,1:T(4,128)S(1)} %get-tuple-element.33), channel_id=1, source_target_pairs={{0,4},{4,8},{8,12},{1,5},{5,9},{9,13},{2,6},{6,10},{10,14},{3,7},{... | collective-permute-start | bytes 393224 | tf_op jit(solution)/shard_map/ppermute | solution.py:17
  27.0 1.3 %collective-permute-start.1 = (f32[4,32,256]{2,0,1:T(4,128)S(1)}, f32[4,32,256]{2,0,1:T(4,128)S(1)}, u32[]{:S(2)}, u32[]{:S(2)}) collective-permute-start(f32[4,32,256]{2,0,1:T(4,128)S(1)} %get-tuple-element.34), channel_id=1, source_target_pairs={{4,0},{8,4},{12,8},{5,1},{9,5},{13,9},{6,2},{10,6},{14,10},{7,3},{... | collective-permute-start | bytes 393224 | tf_op jit(solution)/shard_map/ppermute | solution.py:18
  28.4 2.9 %gather_fusion.3 = f32[384]{0:T(512)S(1)} fusion(f32[16,9]{1,0:T(8,128)S(1)} %get-tuple-element.38, s32[384]{0:T(512)S(1)} %reshape.267), kind=kCustom, calls=%fused_computation.10 | custom fusion | bytes 6144 | tf_op jit(solution)/shard_map/gather | solution.py:87
  31.5 0.9 convolution_divide_fusion
  32.4 4.9 %collective-permute-start.2 = (f32[4,32,256]{2,0,1:T(4,128)S(1)}, f32[4,32,256]{2,0,1:T(4,128)S(1)}, u32[]{:S(2)}, u32[]{:S(2)}) collective-permute-start(f32[4,32,256]{2,0,1:T(4,128)S(1)} %get-tuple-element.31), channel_id=1, source_target_pairs={{0,4},{4,8},{8,12},{1,5},{5,9},{9,13},{2,6},{6,10},{10,14},{3,7},{... | collective-permute-start | bytes 393224 | tf_op jit(solution)/shard_map/ppermute | solution.py:17
  37.3 1.3 %collective-permute-start.3 = (f32[4,32,256]{2,0,1:T(4,128)S(1)}, f32[4,32,256]{2,0,1:T(4,128)S(1)}, u32[]{:S(2)}, u32[]{:S(2)}) collective-permute-start(f32[4,32,256]{2,0,1:T(4,128)S(1)} %get-tuple-element.32), channel_id=1, source_target_pairs={{4,0},{8,4},{12,8},{5,1},{9,5},{13,9},{6,2},{10,6},{14,10},{7,3},{... | collective-permute-start | bytes 393224 | tf_op jit(solution)/shard_map/ppermute | solution.py:18
  38.7 2.9 %gather_fusion.2 = f32[384]{0:T(512)S(1)} fusion(f32[24,9]{1,0:T(8,128)S(1)} %broadcast_select_fusion, s32[384]{0:T(512)S(1)} %reshape.261), kind=kCustom, calls=%fused_computation.9 | custom fusion | bytes 6144 | tf_op jit(solution)/shard_map/gather | solution.py:95
  41.8 0.6 fusion.5
  42.8 1.2 fusion.67
  44.0 0.6 gather_fusion.9
  44.6 0.9 select_bitcast_fusion
  45.5 4.0 %all-to-all-start.1 = ((f32[16,4,8,256]{3,0,2,1:T(8,128)}), f32[16,4,8,256]{3,0,2,1:T(8,128)S(1)}, u32[]{:S(2)}, u32[]{:S(2)}) async-start(f32[16,4,8,256]{3,0,2,1:T(8,128)} %select_bitcast_fusion), calls=%async_computation.1 | async-start | bytes 1048576 | tf_op jit(solution)/shard_map/all_to_all | solution.py:106
  49.6 8.8 %all-to-all-done.1 = f32[16,4,8,256]{3,0,2,1:T(8,128)S(1)} async-done(((f32[16,4,8,256]{3,0,2,1:T(8,128)}), f32[16,4,8,256]{3,0,2,1:T(8,128)S(1)}, u32[]{:S(2)}, u32[]{:S(2)}) %all-to-all-start.1) | async-done | bytes 524320 | tf_op jit(solution)/shard_map/all_to_all | solution.py:106
  58.4 0.6 gather_fusion.10
  59.0 0.9 bitcast_log_fusion
  59.9 46.8 %all-gather.3.cloned.1.call-done = f32[64,4,8,256]{3,0,2,1:T(8,128)} async-done(((f32[16,4,8,256]{3,0,2,1:T(8,128)}), f32[64,4,8,256]{3,0,2,1:T(8,128)}) %all-gather.3.cloned.1.call-update) | async-done | bytes 2097168 | tf_op jit(solution)/shard_map/all_gather | solution.py:108
  106.7 1.9 %reduce_sum.39 = f32[16,4,8,256]{3,0,2,1:T(8,128)S(1)} reduce(f32[4,16,4,8,256]{4,1,0,3,2:T(8,128)} %bitcast.52, f32[]{:T(128)} %constant.110.clone.1), dimensions={0}, to_apply=%region_3.6 | reduce | flops 393216 | bytes 2621444 | tf_op jit(solution)/shard_map/reduce_sum | solution.py:108
  108.7 1.1 copy_multiply_fusion
  (53 shorter events, 2.1 us)
Async XLA Ops:
  6.5 0.7 copy-start
  6.5 7.9 %copy-start.1 = (s32[1,64]{1,0:T(1,128)S(1)}, s32[1,64]{1,0:T(1,128)}, u32[]{:S(2)}) copy-start(s32[1,64]{1,0:T(1,128)} %param.13) | copy-start | bytes 772
  6.5 8.7 %copy-start.3 = (f32[1,4,3,9]{3,1,2,0:T(4,128)S(1)}, f32[1,4,3,9]{3,1,2,0:T(4,128)}, u32[]{:S(2)}) copy-start(f32[1,4,3,9]{3,1,2,0:T(4,128)} %param.11) | copy-start | bytes 1300
  10.2 13.1 %all-to-all-start = ((f32[16,4,8,256]{3,2,0,1:T(8,128)}), f32[16,4,8,256]{3,2,0,1:T(8,128)S(1)}, u32[]{:S(2)}, u32[]{:S(2)}) async-start(f32[16,4,8,256]{3,2,0,1:T(8,128)} %select_bitcast_fusion.2), calls=%async_computation | async-start | bytes 1048576 | tf_op jit(solution)/shard_map/all_to_all | solution.py:64
  25.7 5.7 %collective-permute-start = (f32[4,32,256]{2,0,1:T(4,128)S(1)}, f32[4,32,256]{2,0,1:T(4,128)S(1)}, u32[]{:S(2)}, u32[]{:S(2)}) collective-permute-start(f32[4,32,256]{2,0,1:T(4,128)S(1)} %get-tuple-element.33), channel_id=1, source_target_pairs={{0,4},{4,8},{8,12},{1,5},{5,9},{9,13},{2,6},{6,10},{10,14},{3,7},{... | collective-permute-start | bytes 393224 | tf_op jit(solution)/shard_map/ppermute | solution.py:17
  27.0 4.4 %collective-permute-start.1 = (f32[4,32,256]{2,0,1:T(4,128)S(1)}, f32[4,32,256]{2,0,1:T(4,128)S(1)}, u32[]{:S(2)}, u32[]{:S(2)}) collective-permute-start(f32[4,32,256]{2,0,1:T(4,128)S(1)} %get-tuple-element.34), channel_id=1, source_target_pairs={{4,0},{8,4},{12,8},{5,1},{9,5},{13,9},{6,2},{10,6},{14,10},{7,3},{... | collective-permute-start | bytes 393224 | tf_op jit(solution)/shard_map/ppermute | solution.py:18
  28.4 3.0 %copy-start.4 = (f32[1,16,32,256]{3,2,1,0:T(8,128)S(1)}, f32[1,16,32,256]{3,2,1,0:T(8,128)}, u32[]{:S(2)}) copy-start(f32[1,16,32,256]{3,2,1,0:T(8,128)} %param.10) | copy-start | bytes 1572868
  32.4 9.4 %collective-permute-start.2 = (f32[4,32,256]{2,0,1:T(4,128)S(1)}, f32[4,32,256]{2,0,1:T(4,128)S(1)}, u32[]{:S(2)}, u32[]{:S(2)}) collective-permute-start(f32[4,32,256]{2,0,1:T(4,128)S(1)} %get-tuple-element.31), channel_id=1, source_target_pairs={{0,4},{4,8},{8,12},{1,5},{5,9},{9,13},{2,6},{6,10},{10,14},{3,7},{... | collective-permute-start | bytes 393224 | tf_op jit(solution)/shard_map/ppermute | solution.py:17
  37.3 4.5 %collective-permute-start.3 = (f32[4,32,256]{2,0,1:T(4,128)S(1)}, f32[4,32,256]{2,0,1:T(4,128)S(1)}, u32[]{:S(2)}, u32[]{:S(2)}) collective-permute-start(f32[4,32,256]{2,0,1:T(4,128)S(1)} %get-tuple-element.32), channel_id=1, source_target_pairs={{4,0},{8,4},{12,8},{5,1},{9,5},{13,9},{6,2},{10,6},{14,10},{7,3},{... | collective-permute-start | bytes 393224 | tf_op jit(solution)/shard_map/ppermute | solution.py:18
  45.5 12.8 %all-to-all-start.1 = ((f32[16,4,8,256]{3,0,2,1:T(8,128)}), f32[16,4,8,256]{3,0,2,1:T(8,128)S(1)}, u32[]{:S(2)}, u32[]{:S(2)}) async-start(f32[16,4,8,256]{3,0,2,1:T(8,128)} %select_bitcast_fusion), calls=%async_computation.1 | async-start | bytes 1048576 | tf_op jit(solution)/shard_map/all_to_all | solution.py:106
  49.6 57.2 %all-gather.3.cloned.1.call-start = ((), (), s32[]{:S(2)}) async-start(), calls=%async_computation.2 | async-start | bytes 2621440 | tf_op jit(solution)/shard_map/all_gather | solution.py:108
  59.9 48.8 %copy-start.2 = (f32[16,32,256]{2,1,0:T(8,128)S(1)}, f32[16,32,256]{2,1,0:T(8,128)}, u32[]{:S(2)}) copy-start(f32[16,32,256]{2,1,0:T(8,128)} %param.9) | copy-start | bytes 1572868
Sparse Core Ops, SparseCore 0:
  60.0 46.6 all-gather.2
